TPU v7x, 512 devices: a whole 4x4x16 slice. The times are simulated.
512 devices in a mesh: row: 32 (over x, z_hi, core), col: 16 (over z_lo, y).
Axes of the slice: x: 4, y: 4, z: 16 (z_hi: 4, z_lo: 4; z = z_hi * 4 + z_lo), core: 2. Of those that a mesh axis runs over, the one named last changes fastest.
Arguments:
- images: bfloat16 [32, 128, 128, 256], P('row', 'col'), may hold values from -6 to 6
- weight: bfloat16 [3, 3, 256, 256], P(None, None, None, 'col'), may hold values from -0.125 to 0.125
- norm_gain: float32 [256], replicated, may hold values from 0.5 to 1.5
- cotangent: bfloat16 [32, 128, 128, 256], P('row', 'col'), may hold values from -6 to 6
Outputs:
- features: bfloat16 [32, 128, 128, 256], P('row', 'col')
- input_grad: bfloat16 [32, 128, 128, 256], P('row', 'col')
- weight_grad: float32 [3, 3, 256, 256], P(None, None, None, 'col')
All inputs are finite; a program needn't handle non-finite values.
Results may differ from a plain program's by a relative error of at most 0.013.
Values may be sent and summed in bfloat16 or wider, within the bound.
No kernel may reach another device: no remote copies, remote signals or barrier semaphores. Data moves between devices by JAX's collectives and lax.ppermute only.
A program may use at most 64 MiB of HBM per device.

v0:
```python
import math
import jax
import jax.numpy as jnp
from jax import lax
from jax.sharding import PartitionSpec as P

epsilon = 1e-06
root_half = 0.7071067811865476
norm_const = 0.3989422804014327


def padded_2(value, sides, width):
    for axis, dim in sides:
        peers, length = (lax.axis_size(axis), value.shape[dim])
        up = [(i, (i + 1) % peers) for i in range(peers - 1)]
        down = [(j, i) for i, j in up]
        last = lax.slice_in_dim(value, length - width, length, axis=dim)
        initial = lax.slice_in_dim(value, 0, width, axis=dim)
        before = lax.ppermute(last, axis, up)
        after = lax.ppermute(initial, axis, down)
        value = jnp.concatenate([before, value, after], axis=dim)
    return value


def norm_act(conv_out, upper, norm_gain):
    mean_val = jnp.mean(conv_out, axis=-1, keepdims=True)
    centred = conv_out - mean_val
    variance = jnp.mean(centred * centred, axis=-1, keepdims=True)
    inv_std = lax.rsqrt(variance + epsilon)
    unit = centred * inv_std
    normed = unit * norm_gain
    cdf_val = 0.5 * (1.0 + lax.erf(normed * root_half))
    density = jnp.exp(-0.5 * normed * normed) * norm_const
    outputs = (normed * cdf_val).astype(jnp.bfloat16)
    upstream = upper.astype(jnp.float32) * (cdf_val + normed * density) * norm_gain
    mean_up = jnp.mean(upstream, axis=-1, keepdims=True)
    mean_cross = jnp.mean(upstream * unit, axis=-1, keepdims=True)
    grad_pre = inv_std * (upstream - mean_up - unit * mean_cross)
    return (outputs, grad_pre.astype(jnp.bfloat16))


def window(padded, tap_row, tap_col, tile_rows, tile_cols):
    return padded[:, tap_row : tap_row + tile_rows, tap_col : tap_col + tile_cols, :].reshape(
        -1, padded.shape[-1]
    )


def on_device(images, weight, norm_gain, cotangent):
    img_count, tile_rows, tile_cols, in_chan = images.shape
    whole_kernel = lax.all_gather(weight, "col", axis=3, tiled=True)
    out_chan = whole_kernel.shape[3]
    rimmed = padded_2(images, (("col", 1),), 1)
    padded = jnp.pad(rimmed, ((0, 0), (0, 0), (1, 1), (0, 0)))
    conv_out = jnp.zeros((img_count * tile_rows * tile_cols, out_chan), jnp.float32)
    for tap_row in range(3):
        for tap_col in range(3):
            conv_out = conv_out + jnp.dot(
                window(padded, tap_row, tap_col, tile_rows, tile_cols),
                whole_kernel[tap_row, tap_col],
                preferred_element_type=jnp.float32,
            )
    outputs, grad_pre = norm_act(conv_out, cotangent.reshape(-1, out_chan), norm_gain)
    grad_grid = grad_pre.reshape(img_count, tile_rows, tile_cols, out_chan)
    grad_rimmed = padded_2(grad_grid, (("col", 1),), 1)
    grad_pad = jnp.pad(grad_rimmed, ((0, 0), (0, 0), (1, 1), (0, 0)))
    grad_input = jnp.zeros((img_count * tile_rows * tile_cols, in_chan), jnp.float32)
    pieces = []
    for tap_row in range(3):
        for tap_col in range(3):
            grad_input = grad_input + lax.dot_general(
                window(grad_pad, 2 - tap_row, 2 - tap_col, tile_rows, tile_cols),
                whole_kernel[tap_row, tap_col],
                (((1,), (1,)), ((), ())),
                preferred_element_type=jnp.float32,
            )
            pieces.append(
                lax.dot_general(
                    window(padded, tap_row, tap_col, tile_rows, tile_cols),
                    grad_pre,
                    (((0,), (0,)), ((), ())),
                    preferred_element_type=jnp.float32,
                )
            )
    partial_value = jnp.stack(pieces).reshape(3, 3, in_chan, out_chan)
    col_sum = lax.psum_scatter(partial_value, "col", scatter_dimension=3, tiled=True)
    own_share = lax.psum(col_sum, "row")
    pixels = img_count * lax.axis_size("row") * tile_rows * lax.axis_size("col") * tile_cols
    weight_grad = own_share * (1.0 / math.sqrt(pixels))
    features = outputs.reshape(img_count, tile_rows, tile_cols, out_chan)
    input_grad = grad_input.astype(jnp.bfloat16).reshape(img_count, tile_rows, tile_cols, in_chan)
    return (features, input_grad, weight_grad)


def solution(mesh):
    placed = (
        P("row", "col", None, None),
        P(None, None, None, "col"),
        P(),
        P("row", "col", None, None),
    )
    return jax.shard_map(
        on_device,
        mesh=mesh,
        in_specs=placed,
        out_specs=(
            P("row", "col", None, None),
            P("row", "col", None, None),
            P(None, None, None, "col"),
        ),
        check_vma=False,
    )
```

profile of v0, /device:TPU:1, one launch (start us, length us, event | category | flops | bytes accessed | tf_op | source)
XLA Modules:
  0.0 546.5 jit_solution(15703114254889258676)
XLA Ops:
  7.2 0.7 all-gather.2.cloned.1.call-update
  8.0 0.9 fusion.29
  8.8 4.0 collective-permute-start
  12.9 1.3 collective-permute-start.1
  14.2 3.7 collective-permute-done.1
  17.9 1.2 select_maximum_fusion.2
  19.1 1.0 pad_maximum_fusion.2
  20.2 1.4 fusion.27
  21.5 70.6 %all-gather.2.cloned.1.call-done = bf16[3,3,256,256]{2,3,1,0:T(8,128)(2,1)} async-done(((bf16[3,3,256,16]{2,3,1,0:T(8,128)(2,1)}), bf16[3,3,256,256]{2,3,1,0:T(8,128)(2,1)}) %all-gather.2.cloned.1.call-update) | async-done | bytes 1179664 | tf_op jit(solution)/shard_map/all_gather | solution.py:50
  92.2 1.4 fusion.21
  93.5 0.3 fusion.23
  93.9 0.3 convolution_add_fusion.13
  94.3 0.7 copy-done.6
  94.9 0.3 convolution_add_fusion.12
  95.3 0.3 convolution_add_fusion.11
  95.7 0.3 convolution_add_fusion.10
  96.0 0.7 copy-done.4
  96.7 0.3 convolution_add_fusion.9
  97.1 0.3 convolution_add_fusion.8
  97.4 0.7 copy-done.7
  98.1 0.4 fusion.30
  98.5 0.4 multiply_reduce_fusion.1
  98.9 0.6 copy-done.9
  99.6 1.9 fusion.24
  101.5 0.8 multiply_convert_fusion
  102.3 1.0 fusion.12
  103.4 1.1 fusion.11
  104.4 1.1 fusion.10
  105.5 1.0 fusion.9
  106.5 1.0 fusion.8
  107.6 1.1 fusion.7
  108.6 1.0 fusion.6
  109.6 1.0 fusion.5
  110.7 1.0 fusion.4
  111.7 3.1 copy.8
  115.0 2.7 collective-permute-start.2
  117.7 1.3 collective-permute-start.3
  119.0 3.7 collective-permute-done.3
  122.9 0.9 pad_maximum_fusion
  123.8 0.4 fusion.26
  124.2 0.3 fusion.20
  124.8 0.3 convolution_add_fusion.6
  125.4 0.3 convolution_add_fusion.4
  126.3 0.3 convolution_add_fusion.1
  126.6 79.9 %reduce-scatter.2.cloned.1.call-done = f32[3,3,256,16]{2,3,1,0:T(8,128)} async-done(((f32[3,3,256,256]{2,3,1,0:T(8,128)}), f32[3,3,256,16]{2,3,1,0:T(8,128)}) %reduce-scatter.2.cloned.1.call-update) | async-done | bytes 147472 | tf_op jit(solution)/shard_map/reduce_scatter | solution.py:85
  206.6 2.1 fusion.3
  208.7 329.7 %all-reduce.4.cloned.1.call-done = f32[3,3,256,16]{2,3,1,0:T(8,128)} async-done(((f32[3,3,256,16]{2,3,1,0:T(8,128)}), f32[3,3,256,16]{2,3,1,0:T(8,128)}) %all-reduce.4.cloned.1.call-update) | async-done | bytes 147472 | tf_op jit(solution)/shard_map/psum | solution.py:86
  538.4 1.6 broadcast_multiply_fusion
  (34 shorter events, 1.7 us)
Async XLA Ops:
  7.2 12.0 %copy-start = (bf16[1,8,128,256]{3,2,1,0:T(8,128)(2,1)S(1)}, bf16[1,8,128,256]{3,2,1,0:T(8,128)(2,1)}, u32[]{:S(2)}) copy-start(bf16[1,8,128,256]{3,2,1,0:T(8,128)(2,1)} %param.4) | copy-start | bytes 1572868
  7.2 85.0 %all-gather.2.cloned.1.call-start = ((), (), s32[]{:S(2)}) async-start(), calls=%async_computation.1 | async-start | bytes 1253376 | tf_op jit(solution)/shard_map/all_gather | solution.py:50
  7.9 198.6 %reduce-scatter.2.cloned.1.call-start = ((), (), s32[]{:S(2)}) async-start(), calls=%async_computation.2 | async-start | bytes 2506752 | tf_op jit(solution)/shard_map/reduce_scatter | solution.py:85
  8.8 5.4 collective-permute-start
  12.9 5.0 collective-permute-start.1
  21.5 75.5 %copy-start.2 = (bf16[1,8,128,256]{3,2,1,0:T(8,128)(2,1)}, bf16[1,8,128,256]{3,2,1,0:T(8,128)(2,1)S(1)}, u32[]{:S(2)}) copy-start(bf16[1,8,128,256]{3,2,1,0:T(8,128)(2,1)S(1)} %get-tuple-element.13) | copy-start | bytes 1572868
  92.2 1.4 copy-start.1
  92.2 1.7 copy-start.8
  93.9 1.0 copy-start.6
  94.2 1.1 copy-start.5
  95.7 1.0 copy-start.4
  97.0 1.0 copy-start.7
  98.1 0.8 copy-start.10
  98.5 1.0 copy-start.9
  106.5 2.1 copy-start.3
  114.9 423.5 %all-reduce.4.cloned.1.call-start = ((), (), s32[]{:S(2)}) async-start(), calls=%async_computation.3 | async-start | bytes 294912 | tf_op jit(solution)/shard_map/psum | solution.py:86
  115.0 4.1 collective-permute-start.2
  117.7 5.0 collective-permute-start.3
Sparse Core Ops, SparseCore 0:
  10.1 82.0 all-gather.1
  115.0 91.4 reduce-scatter.1
  209.5 328.8 all-reduce.3
where the time goes:
time: 547 us
  waiting for transfers between devices  488 us (89%)
  matrix products  18 us (3%)
  between operations  14 us (3%)
  starting transfers between devices  9.47 us (2%)
  local copies, waits for them, and re-layouts  8.58 us (2%)
  other arithmetic  8.02 us (1%)
    psum x1, waiting for transfers between devices, on_device(): own_share = lax.psum(col_sum, 'row')  330 us
    reduce_scatter x1, waiting for transfers between devices, on_device(): lax.psum_scatter(partial_value, 'col', scatter_dimension=3, tiled=True)  79.9 us
    all_gather x1, waiting for transfers between devices, on_device(): whole_kernel = lax.all_gather(weight, 'col', axis=3, tiled=True)  70.6 us
  transfers between devices with their start and end apart: 7, of which 5 were waited for; matrix products, arithmetic and copies ran while one was open for 2% of the time, Pallas kernels for 0%

commit v1 on v0

--- a/solution.py
+++ b/solution.py
@@ -47,7 +47,9 @@
 
 def on_device(images, weight, norm_gain, cotangent):
     img_count, tile_rows, tile_cols, in_chan = images.shape
-    whole_kernel = lax.all_gather(weight, "col", axis=3, tiled=True)
+    whole_kernel = jnp.concatenate(
+        lax.all_to_all(jnp.stack([weight] * lax.axis_size("col")), "col", 0, 0), axis=3
+    )
     out_chan = whole_kernel.shape[3]
     rimmed = padded_2(images, (("col", 1),), 1)
     padded = jnp.pad(rimmed, ((0, 0), (0, 0), (1, 1), (0, 0)))

time: 547 us -> 499 us (0.912)
  waiting for transfers between devices: 488 us -> 432 us
  starting transfers between devices: 9.47 us -> 17.2 us
    all_gather x1 -> x0, waiting for transfers between devices: 70.6 us -> none  [on_device(): whole_kernel = lax.all_gather(weight, 'col', axis=3, tiled=True)]
    all_to_all x0 -> x1, waiting for transfers between devices: none -> 12.5 us  [on_device(): lax.all_to_all(jnp.stack([weight] * lax.axis_size('col')), 'col', 0, 0)]
    all_to_all x0 -> x1, starting transfers between devices: none -> 9.32 us  [on_device(): lax.all_to_all(jnp.stack([weight] * lax.axis_size('col')), 'col', 0, 0)]
  transfers between devices with their start and end apart: 7 -> 7, of which waited for: 5 -> 6; matrix products, arithmetic and copies ran while one was open for 2% -> 2% of each run, Pallas kernels for 0% -> 0%
where the time goes in v1:
time: 499 us
  waiting for transfers between devices  432 us (87%)
  starting transfers between devices  17.2 us (3%)
  matrix products  17 us (3%)
  between operations  14.3 us (3%)
  local copies, waits for them, and re-layouts  11.3 us (2%)
  other arithmetic  7.06 us (1%)
    psum x1, waiting for transfers between devices, on_device(): own_share = lax.psum(col_sum, 'row')  330 us
    reduce_scatter x1, waiting for transfers between devices, on_device(): lax.psum_scatter(partial_value, 'col', scatter_dimension=3, tiled=True)  79.7 us
    all_to_all x1, waiting for transfers between devices, on_device(): lax.all_to_all(jnp.stack([weight] * lax.axis_size('col')), 'col', 0, 0)  12.5 us
  transfers between devices with their start and end apart: 7, of which 6 were waited for; matrix products, arithmetic and copies ran while one was open for 2% of the time, Pallas kernels for 0%

profile of v1, /device:TPU:1, one launch (start us, length us, event | category | flops | bytes accessed | tf_op | source)
XLA Modules:
  0.0 498.7 jit_solution(3519851480546744558)
XLA Ops:
  7.2 2.0 stack.22
  9.2 9.3 %all-to-all-start = ((bf16[16,3,3,256,16]{3,4,2,1,0:T(8,128)(2,1)}), bf16[16,3,3,256,16]{3,4,2,1,0:T(8,128)(2,1)S(1)}, u32[]{:S(2)}, u32[]{:S(2)}) async-start(bf16[16,3,3,256,16]{3,4,2,1,0:T(8,128)(2,1)} %stack.22), calls=%async_computation | async-start | bytes 2359296 | tf_op jit(solution)/shard_map/all_to_all | solution.py:51
  18.6 3.3 collective-permute-start
  21.8 1.3 collective-permute-start.1
  23.1 1.2 collective-permute-done
  24.4 3.0 collective-permute-done.1
  27.5 1.1 pad_maximum_fusion.2
  28.6 1.6 fusion.27
  30.3 12.5 %all-to-all-done = bf16[16,3,3,256,16]{3,4,2,1,0:T(8,128)(2,1)S(1)} async-done(((bf16[16,3,3,256,16]{3,4,2,1,0:T(8,128)(2,1)}), bf16[16,3,3,256,16]{3,4,2,1,0:T(8,128)(2,1)S(1)}, u32[]{:S(2)}, u32[]{:S(2)}) %all-to-all-start) | async-done | bytes 1179680 | tf_op jit(solution)/shard_map/all_to_all | solution.py:51
  42.9 0.9 copy-done.1
  43.8 0.3 fusion.21
  44.1 0.3 fusion.23
  44.5 0.4 copy-done.7
  44.8 0.3 convolution_add_fusion.13
  45.2 0.4 copy-done.5
  45.5 0.3 convolution_add_fusion.12
  45.9 0.4 copy-done.4
  46.2 0.3 convolution_add_fusion.11
  46.6 0.3 convolution_add_fusion.10
  46.9 0.7 copy-done.3
  47.6 0.3 convolution_add_fusion.9
  48.0 0.3 convolution_add_fusion.8
  48.3 0.7 copy-done.6
  49.0 0.4 fusion.30
  49.5 0.4 multiply_reduce_fusion.1
  49.9 0.6 copy-done.8
  50.5 1.9 fusion.24
  52.4 0.9 multiply_convert_fusion
  53.3 1.0 fusion.12
  54.3 1.0 fusion.11
  55.4 1.1 fusion.10
  56.4 1.0 fusion.9
  57.5 1.1 fusion.8
  58.5 1.1 fusion.7
  59.6 1.0 fusion.6
  60.6 1.0 fusion.5
  61.6 1.0 fusion.4
  62.7 3.1 copy.14
  65.9 1.9 collective-permute-start.2
  67.8 1.3 collective-permute-start.3
  69.1 5.7 %collective-permute-done.3 = bf16[1,1,128,256]{3,2,1,0:T(8,128)(2,1)S(1)} collective-permute-done((bf16[1,1,128,256]{3,2,1,0:T(8,128)(2,1)S(1)}, bf16[1,1,128,256]{3,2,1,0:T(8,128)(2,1)S(1)}, u32[]{:S(2)}, u32[]{:S(2)}) %collective-permute-start.3) | collective-permute-done | bytes 65568 | tf_op jit(solution)/shard_map/ppermute | solution.py:20
  75.0 0.9 pad_maximum_fusion
  75.9 0.4 fusion.26
  76.3 0.3 fusion.20
  78.8 79.7 %reduce-scatter.2.cloned.1.call-done = f32[3,3,256,16]{2,3,1,0:T(8,128)} async-done(((f32[3,3,256,256]{2,3,1,0:T(8,128)}), f32[3,3,256,16]{2,3,1,0:T(8,128)}) %reduce-scatter.2.cloned.1.call-update) | async-done | bytes 147472 | tf_op jit(solution)/shard_map/reduce_scatter | solution.py:87
  158.5 2.1 fusion.3
  160.7 329.6 %all-reduce.4.cloned.1.call-done = f32[3,3,256,16]{2,3,1,0:T(8,128)} async-done(((f32[3,3,256,16]{2,3,1,0:T(8,128)}), f32[3,3,256,16]{2,3,1,0:T(8,128)}) %all-reduce.4.cloned.1.call-update) | async-done | bytes 147472 | tf_op jit(solution)/shard_map/psum | solution.py:88
  490.3 1.6 broadcast_multiply_fusion
  (33 shorter events, 2.8 us)
Async XLA Ops:
  9.2 9.4 %copy-start = (bf16[1,8,128,256]{3,2,1,0:T(8,128)(2,1)S(1)}, bf16[1,8,128,256]{3,2,1,0:T(8,128)(2,1)}, u32[]{:S(2)}) copy-start(bf16[1,8,128,256]{3,2,1,0:T(8,128)(2,1)} %param.4) | copy-start | bytes 1572868
  9.2 33.6 %all-to-all-start = ((bf16[16,3,3,256,16]{3,4,2,1,0:T(8,128)(2,1)}), bf16[16,3,3,256,16]{3,4,2,1,0:T(8,128)(2,1)S(1)}, u32[]{:S(2)}, u32[]{:S(2)}) async-start(bf16[16,3,3,256,16]{3,4,2,1,0:T(8,128)(2,1)} %stack.22), calls=%async_computation | async-start | bytes 2359296 | tf_op jit(solution)/shard_map/all_to_all | solution.py:51
  18.5 140.0 %reduce-scatter.2.cloned.1.call-start = ((), (), s32[]{:S(2)}) async-start(), calls=%async_computation.2 | async-start | bytes 2506752 | tf_op jit(solution)/shard_map/reduce_scatter | solution.py:87
  18.6 5.8 %collective-permute-start = (bf16[1,1,128,256]{3,2,1,0:T(8,128)(2,1)S(1)}, bf16[1,1,128,256]{3,2,1,0:T(8,128)(2,1)S(1)}, u32[]{:S(2)}, u32[]{:S(2)}) collective-permute-start(bf16[1,1,128,256]{3,2,1,0:T(8,128)(2,1)S(1)} %get-tuple-element.25), channel_id=1, source_target_pairs={{0,1},{1,2},{2,3},{3,4},{4,5},{5,6},{6,7},{7,8},{8,9},{9,10},{10,1... | collective-permute-start | bytes 196616 | tf_op jit(solution)/shard_map/ppermute | solution.py:19
  21.8 5.5 %collective-permute-start.1 = (bf16[1,1,128,256]{3,2,1,0:T(8,128)(2,1)S(1)}, bf16[1,1,128,256]{3,2,1,0:T(8,128)(2,1)S(1)}, u32[]{:S(2)}, u32[]{:S(2)}) collective-permute-start(bf16[1,1,128,256]{3,2,1,0:T(8,128)(2,1)S(1)} %get-tuple-element.26), channel_id=1, source_target_pairs={{1,0},{2,1},{3,2},{4,3},{5,4},{6,5},{7,6},{8,7},{9,8},{10,9},{11,1... | collective-permute-start | bytes 196616 | tf_op jit(solution)/shard_map/ppermute | solution.py:20
  42.7 1.0 copy-start.1
  43.8 1.0 copy-start.7
  44.5 1.1 copy-start.5
  45.2 1.1 copy-start.4
  46.6 1.0 copy-start.3
  46.9 1.1 copy-start.2
  47.9 1.1 copy-start.6
  49.0 0.8 copy-start.9
  49.4 1.0 copy-start.8
  65.8 424.5 %all-reduce.4.cloned.1.call-start = ((), (), s32[]{:S(2)}) async-start(), calls=%async_computation.3 | async-start | bytes 294912 | tf_op jit(solution)/shard_map/psum | solution.py:88
  65.9 3.3 collective-permute-start.2
  67.8 7.1 %collective-permute-start.3 = (bf16[1,1,128,256]{3,2,1,0:T(8,128)(2,1)S(1)}, bf16[1,1,128,256]{3,2,1,0:T(8,128)(2,1)S(1)}, u32[]{:S(2)}, u32[]{:S(2)}) collective-permute-start(bf16[1,1,128,256]{3,2,1,0:T(8,128)(2,1)S(1)} %get-tuple-element.22), channel_id=1, source_target_pairs={{1,0},{2,1},{3,2},{4,3},{5,4},{6,5},{7,6},{8,7},{9,8},{10,9},{11,1... | collective-permute-start | bytes 196616 | tf_op jit(solution)/shard_map/ppermute | solution.py:20
Sparse Core Ops, SparseCore 0:
  65.9 92.5 reduce-scatter.1
  161.4 328.8 all-reduce.3

commit v2 on v0

--- a/solution.py
+++ b/solution.py
@@ -83,7 +83,7 @@
             )
     partial_value = jnp.stack(pieces).reshape(3, 3, in_chan, out_chan)
     col_sum = lax.psum_scatter(partial_value, "col", scatter_dimension=3, tiled=True)
-    own_share = lax.psum(col_sum, "row")
+    own_share = jnp.sum(lax.all_gather(col_sum, "row"), axis=0)
     pixels = img_count * lax.axis_size("row") * tile_rows * lax.axis_size("col") * tile_cols
     weight_grad = own_share * (1.0 / math.sqrt(pixels))
     features = outputs.reshape(img_count, tile_rows, tile_cols, out_chan)

time: 547 us -> 422 us (0.77)
  waiting for transfers between devices: 488 us -> 357 us
  local copies, waits for them, and re-layouts: 8.58 us -> 14.3 us
    psum x1 -> x0, waiting for transfers between devices: 330 us -> none  [on_device(): own_share = lax.psum(col_sum, 'row')]
    unnamed x3 -> x4, waiting for transfers between devices: 0.71 us -> 181 us
    all_gather x0 -> x1, waiting for transfers between devices: none -> 97.9 us  [on_device(): own_share = jnp.sum(lax.all_gather(col_sum, 'row'), axis=0)]
    reduce_scatter x1 -> x0, waiting for transfers between devices: 79.9 us -> none  [on_device(): lax.psum_scatter(partial_value, 'col', scatter_dimension=3, tiled=True)]
  transfers between devices with their start and end apart: 7 -> 7, of which waited for: 5 -> 6; matrix products, arithmetic and copies ran while one was open for 2% -> 2% of each run, Pallas kernels for 0% -> 0%
where the time goes in v2:
time: 422 us; the launch traced here: 421 us
  waiting for transfers between devices  357 us (85%)
  matrix products  17 us (4%)
  between operations  14.7 us (3%)
  local copies, waits for them, and re-layouts  14.3 us (3%)
  starting transfers between devices  9.56 us (2%)
  other arithmetic  8.47 us (2%)
    unnamed x4, waiting for transfers between devices  181 us
    all_gather x1, waiting for transfers between devices, on_device(): own_share = jnp.sum(lax.all_gather(col_sum, 'row'), axis=0)  97.9 us
    all_gather x1, waiting for transfers between devices, on_device(): whole_kernel = lax.all_gather(weight, 'col', axis=3, tiled=True)  70.7 us
    dot_general x9, matrix products, on_device(): lax.dot_general(window(padded, tap_row, tap_col, tile_rows, tile_cols), g...  9.41 us
  transfers between devices with their start and end apart: 7, of which 6 were waited for; matrix products, arithmetic and copies ran while one was open for 2% of the time, Pallas kernels for 0%

profile of v2, /device:TPU:1, one launch (start us, length us, event | category | flops | bytes accessed | tf_op | source)
XLA Modules:
  0.0 421.2 jit_solution(3017448570923510313)
XLA Ops:
  7.2 0.7 all-gather.4.cloned.1.call-update
  8.0 0.9 fusion.29
  8.8 4.0 collective-permute-start
  12.9 1.3 collective-permute-start.1
  14.2 3.7 collective-permute-done.1
  17.9 1.2 select_maximum_fusion.2
  19.1 1.0 pad_maximum_fusion.2
  20.2 1.4 fusion.27
  21.5 70.7 %all-gather.4.cloned.1.call-done = bf16[3,3,256,256]{2,3,1,0:T(8,128)(2,1)} async-done(((bf16[3,3,256,16]{2,3,1,0:T(8,128)(2,1)}), bf16[3,3,256,256]{2,3,1,0:T(8,128)(2,1)}) %all-gather.4.cloned.1.call-update) | async-done | bytes 1179664 | tf_op jit(solution)/shard_map/all_gather | solution.py:50
  92.2 1.4 fusion.21
  93.5 0.3 fusion.23
  93.9 0.3 convolution_add_fusion.13
  94.3 0.7 copy-done.6
  94.9 0.3 convolution_add_fusion.12
  95.3 0.3 convolution_add_fusion.11
  95.7 0.3 convolution_add_fusion.10
  96.0 0.7 copy-done.4
  96.7 0.3 convolution_add_fusion.9
  97.1 0.3 convolution_add_fusion.8
  97.4 0.7 copy-done.7
  98.1 0.4 fusion.30
  98.5 0.4 multiply_reduce_fusion.1
  98.9 0.6 copy-done.9
  99.6 1.9 fusion.24
  101.5 0.8 multiply_convert_fusion
  102.3 1.0 fusion.12
  103.4 1.0 fusion.11
  104.4 1.0 fusion.10
  105.5 1.0 fusion.9
  106.5 1.1 fusion.8
  107.5 1.0 fusion.7
  108.6 1.1 fusion.6
  109.7 1.0 fusion.5
  110.7 1.1 fusion.4
  111.8 4.6 %copy.9 = f32[3,3,256,256]{2,1,0,3:T(4,128)} copy(f32[3,3,256,256]{3,2,1,0:T(8,128)} %bitcast.40) | data formatting | bytes 4718592 | tf_op jit(solution)/shard_map/reshape | solution.py:84
  116.4 1.3 dynamic-slice
  118.3 180.5 %all-reduce.5.cloned.1.call-done = f32[3,3,256,256]{2,1,0,3:T(4,128)} async-done(((f32[3,3,256,256]{2,1,0,3:T(4,128)}), f32[3,3,256,256]{2,1,0,3:T(4,128)}) %all-reduce.5.cloned.1.call-update) | async-done | bytes 2359312
  298.8 1.0 constant_dynamic-slice_fusion
  299.8 0.7 copy.10
  300.5 2.8 collective-permute-start.2
  303.4 1.3 collective-permute-start.3
  304.9 3.5 collective-permute-done.3
  308.6 0.4 fusion.26
  311.5 1.1 fusion.3
  312.6 97.9 %all-gather.6.cloned.1.call-done = f32[96,3,256,16]{2,3,1,0:T(8,128)} async-done(((f32[3,3,256,16]{2,3,1,0:T(8,128)}), f32[96,3,256,16]{2,3,1,0:T(8,128)}) %all-gather.6.cloned.1.call-update) | async-done | bytes 4718608 | tf_op jit(solution)/shard_map/all_gather | solution.py:86
  410.5 2.7 reduce_sum.49
  413.2 0.4 copy.14
  413.7 1.0 copy.12
  (40 shorter events, 3.3 us)
Async XLA Ops:
  7.2 12.0 %copy-start = (bf16[1,8,128,256]{3,2,1,0:T(8,128)(2,1)S(1)}, bf16[1,8,128,256]{3,2,1,0:T(8,128)(2,1)}, u32[]{:S(2)}) copy-start(bf16[1,8,128,256]{3,2,1,0:T(8,128)(2,1)} %param.4) | copy-start | bytes 1572868
  7.2 85.0 %all-gather.4.cloned.1.call-start = ((), (), s32[]{:S(2)}) async-start(), calls=%async_computation | async-start | bytes 1253376 | tf_op jit(solution)/shard_map/all_gather | solution.py:50
  7.9 290.9 %all-reduce.5.cloned.1.call-start = ((), (), s32[]{:S(2)}) async-start(), calls=%async_computation.2 | async-start | bytes 6291456
  8.8 5.4 %collective-permute-start = (bf16[1,1,128,256]{3,2,1,0:T(8,128)(2,1)S(1)}, bf16[1,1,128,256]{3,2,1,0:T(8,128)(2,1)S(1)}, u32[]{:S(2)}, u32[]{:S(2)}) collective-permute-start(bf16[1,1,128,256]{3,2,1,0:T(8,128)(2,1)S(1)} %get-tuple-element.28), channel_id=1, source_target_pairs={{0,1},{1,2},{2,3},{3,4},{4,5},{5,6},{6,7},{7,8},{8,9},{9,10},{10,1... | collective-permute-start | bytes 196616 | tf_op jit(solution)/shard_map/ppermute | solution.py:19
  12.9 5.0 %collective-permute-start.1 = (bf16[1,1,128,256]{3,2,1,0:T(8,128)(2,1)S(1)}, bf16[1,1,128,256]{3,2,1,0:T(8,128)(2,1)S(1)}, u32[]{:S(2)}, u32[]{:S(2)}) collective-permute-start(bf16[1,1,128,256]{3,2,1,0:T(8,128)(2,1)S(1)} %get-tuple-element.29), channel_id=1, source_target_pairs={{1,0},{2,1},{3,2},{4,3},{5,4},{6,5},{7,6},{8,7},{9,8},{10,9},{11,1... | collective-permute-start | bytes 196616 | tf_op jit(solution)/shard_map/ppermute | solution.py:20
  21.5 75.5 %copy-start.2 = (bf16[1,8,128,256]{3,2,1,0:T(8,128)(2,1)}, bf16[1,8,128,256]{3,2,1,0:T(8,128)(2,1)S(1)}, u32[]{:S(2)}) copy-start(bf16[1,8,128,256]{3,2,1,0:T(8,128)(2,1)S(1)} %get-tuple-element.16) | copy-start | bytes 1572868
  92.2 1.4 copy-start.1
  92.2 1.7 copy-start.8
  93.9 1.0 copy-start.6
  94.2 1.1 copy-start.5
  95.7 1.0 copy-start.4
  97.0 1.0 copy-start.7
  98.1 0.8 copy-start.10
  98.5 1.0 copy-start.9
  106.5 2.1 copy-start.3
  116.3 294.1 %all-gather.6.cloned.1.call-start = ((), (), s32[]{:S(2)}) async-start(), calls=%async_computation.1 | async-start | bytes 4866048 | tf_op jit(solution)/shard_map/all_gather | solution.py:86
  300.5 4.4 %collective-permute-start.2 = (bf16[1,1,128,256]{3,2,1,0:T(8,128)(2,1)S(1)}, bf16[1,1,128,256]{3,2,1,0:T(8,128)(2,1)S(1)}, u32[]{:S(2)}, u32[]{:S(2)}) collective-permute-start(bf16[1,1,128,256]{3,2,1,0:T(8,128)(2,1)S(1)} %get-tuple-element.24), channel_id=1, source_target_pairs={{0,1},{1,2},{2,3},{3,4},{4,5},{5,6},{6,7},{7,8},{8,9},{9,10},{10,1... | collective-permute-start | bytes 196616 | tf_op jit(solution)/shard_map/ppermute | solution.py:19
  303.4 5.0 %collective-permute-start.3 = (bf16[1,1,128,256]{3,2,1,0:T(8,128)(2,1)S(1)}, bf16[1,1,128,256]{3,2,1,0:T(8,128)(2,1)S(1)}, u32[]{:S(2)}, u32[]{:S(2)}) collective-permute-start(bf16[1,1,128,256]{3,2,1,0:T(8,128)(2,1)S(1)} %get-tuple-element.25), channel_id=1, source_target_pairs={{1,0},{2,1},{3,2},{4,3},{5,4},{6,5},{7,6},{8,7},{9,8},{10,9},{11,1... | collective-permute-start | bytes 196616 | tf_op jit(solution)/shard_map/ppermute | solution.py:20
Sparse Core Ops, SparseCore 0:
  10.1 82.0 all-gather.3
  116.5 182.3 all-reduce.4
  302.5 107.8 all-gather.5
